TPU v7x, 512 devices: a whole 4x8x8 slice. The times are simulated.
512 devices in a mesh: grp: 16 (over z, core), dev: 32 (over x, y).
Axes of the slice: x: 4, y: 8, z: 8, core: 2. Of those that a mesh axis runs over, the one named last changes fastest.
Arguments:
- ssm_input: bfloat16 [4096, 4096], P('grp', 'dev'), may hold values from -6 to 6
- gate_input: bfloat16 [4096, 4096], P('grp', 'dev'), may hold values from -6 to 6
- step_size: float32 [4096, 64], P('grp', 'dev'), may hold values from 6.1035156e-05 to 0.3375
- decay_rate: float32 [64], P('dev'), may hold values from 0.5 to 2
- in_coeff: bfloat16 [4096, 128], P('grp'), may hold values from -6 to 6
- out_coeff: bfloat16 [4096, 128], P('grp'), may hold values from -6 to 6
- skip_gain: float32 [64], P('dev'), may hold values from 0.5 to 3
- norm_gain: float32 [4096], P('dev'), may hold values from 0.5 to 1.5
- out_proj: bfloat16 [4096, 2048], P(None, 'dev'), may hold values from -0.09375 to 0.09375
- residual: bfloat16 [4096, 2048], P(('grp', 'dev')), may hold values from -6 to 6
- ffn_gain: float32 [2048], replicated, may hold values from 0.5 to 1.5
- router: float32 [2048, 16], replicated, may hold values from -0.125 to 0.125
- routes: int32 [4096, 2], P(('grp', 'dev')), may hold values from 0 to 15, all different within a row; in each aligned block of 8 rows (0 to 7, 8 to 15, ...) at most 2 rows name the same one
- gate_weight: bfloat16 [16, 2048, 8192], P('grp', None, 'dev'), may hold values from -0.125 to 0.125
- up_weight: bfloat16 [16, 2048, 8192], P('grp', None, 'dev'), may hold values from -0.125 to 0.125
- down_weight: bfloat16 [16, 8192, 2048], P('grp', 'dev'), may hold values from -0.0625 to 0.0625
Outputs:
- moe_out: bfloat16 [4096, 2048], P(('grp', 'dev'))
Inputs may be any that keep to these rules, and one draw needn't show every extreme that they name: `routes`: each row names two different experts; among the 8 rows of one dispatch block of consecutive tokens no expert is named more than 2 times, a bound that some block reaches.
All inputs are finite; a program needn't handle non-finite values.
Results may differ from a plain program's by a relative error of at most 0.012.
Values may be sent and summed in bfloat16 or wider, within the bound.
No kernel may reach another device: no remote copies, remote signals or barrier semaphores. Data moves between devices by JAX's collectives and lax.ppermute only.
A program may use at most 64 MiB of HBM per device.

v0:
```python
import jax
import jax.numpy as jnp
from jax import lax
from jax.sharding import Mesh
from jax.sharding import PartitionSpec as P

DEV = ("dev_0", "dev_1")
GRP_DEV = ("grp", "dev_0", "dev_1")
EPSILON = 1e-05
HIGHEST_PREC = lax.Precision.HIGHEST


def side_by_side(arrays, axis, dim, along):
    columns = [a.reshape(*a.shape[:along], -1) for a in arrays]
    both = jnp.concatenate(columns, axis=along)
    filled, at, finished = (lax.all_gather(both, axis, axis=dim, tiled=True), 0, [])
    for a, column in zip(arrays, columns):
        piece = filled[..., at : at + column.shape[along]]
        finished.append(piece.reshape(*piece.shape[:along], *a.shape[along:]))
        at += column.shape[along]
    return tuple(finished)


def sent_to_all(shard, axis):
    peers = lax.axis_size(axis)
    return lax.all_to_all(
        jnp.broadcast_to(shard[None], (peers, *shard.shape)), axis, 0, 0, tiled=True
    )


def of_everyone(shard, axis):
    everything = sent_to_all(shard, axis)
    return jnp.sum(everything, axis=0)


def in_order(tiles, dim):
    dims = list(tiles.shape[1:])
    dims[dim] *= tiles.shape[0]
    return jnp.moveaxis(tiles, 0, dim).reshape(dims)


def collect(shard, axis, dim):
    return in_order(sent_to_all(shard, axis), dim)


def sum_by_axis(terms, axes):
    total = terms.astype(jnp.bfloat16)
    total = lax.psum_scatter(total, axes, scatter_dimension=0, tiled=True)
    return total.astype(jnp.float32)


def rms_scale(values, gain_vec):
    return (
        values * lax.rsqrt(jnp.mean(values * values, axis=-1, keepdims=True) + EPSILON) * gain_vec
    )


def slot_tables(routes_block, expert_count, slot_cap):
    blocks, row_total = (routes_block.shape[0], routes_block.shape[1])
    flat_routes = routes_block.reshape(blocks, row_total * 2)
    onehot = (
        flat_routes[:, :, None] == jnp.arange(expert_count, dtype=jnp.int32)[None, None, :]
    ).astype(jnp.int32)
    earlier = jnp.cumsum(onehot, axis=1) - onehot
    slot_rank = jnp.sum(earlier * onehot, axis=2)
    slot_index = (flat_routes * slot_cap + slot_rank).reshape(blocks, row_total, 2)
    placed = (
        slot_index[:, :, :, None]
        == jnp.arange(expert_count * slot_cap, dtype=jnp.int32)[None, None, None, :]
    )
    return placed.astype(jnp.float32)


def shards(
    ssm_input,
    gate_input,
    step_size,
    decay_rate,
    in_coeff,
    out_coeff,
    skip_gain,
    norm_gain,
    out_proj,
    residual,
    ffn_gain,
    router,
    routes,
    gate_weight,
    up_weight,
    down_weight,
):
    tok_rows = ssm_input.shape[0]
    head_count = step_size.shape[1]
    head_width = ssm_input.shape[1] // head_count
    dev_count = lax.axis_size(DEV)
    inner_dim = ssm_input.shape[1] * dev_count
    block_rows = residual.shape[0]
    model_dim = residual.shape[1]
    experts = lax.axis_size("grp")
    slot_cap = max(2, 4 * block_rows // experts)
    group_slots = experts * slot_cap
    inputs_f = ssm_input.astype(jnp.float32).reshape(tok_rows, head_count, head_width)
    in_float = in_coeff.astype(jnp.float32)
    out_float = out_coeff.astype(jnp.float32)
    log_rate = -(step_size * decay_rate[None, :])
    cumulative = jnp.cumsum(log_rate, axis=0)
    causal = (jnp.arange(tok_rows)[:, None] >= jnp.arange(tok_rows)[None, :])[:, :, None]
    spread = cumulative[:, None, :] - cumulative[None, :, :]
    decay_pair = jnp.where(causal, jnp.exp(jnp.where(causal, spread, 0.0)), 0.0)
    scores = jnp.dot(out_coeff, in_coeff.T, preferred_element_type=jnp.float32)
    mixing = decay_pair * scores[:, :, None] * step_size[None, :, :]
    inside = jnp.einsum("tuh,uhp->thp", mixing, inputs_f, precision=HIGHEST_PREC)
    to_end = jnp.exp(cumulative[-1][None, :] - cumulative) * step_size
    own_state = jnp.einsum("uh,uhp,un->hpn", to_end, inputs_f, in_float, precision=HIGHEST_PREC)
    own_log = cumulative[-1]
    group_logs, group_states = tuple(
        (
            part.astype(jnp.float32)
            for part in side_by_side(
                (own_log[None].astype(jnp.bfloat16), own_state[None].astype(jnp.bfloat16)),
                "grp",
                0,
                2,
            )
        )
    )
    group_index = jnp.arange(group_logs.shape[0])
    my_group = lax.axis_index("grp")
    inclusive = jnp.cumsum(group_logs, axis=0)
    exclusive = inclusive - group_logs
    before_me = jnp.sum(jnp.where((group_index == my_group)[:, None], exclusive, 0.0), axis=0)
    earlier_mask = (group_index < my_group)[:, None]
    weighting = jnp.where(
        earlier_mask, jnp.exp(jnp.where(earlier_mask, before_me[None, :] - inclusive, 0.0)), 0.0
    )
    entering = jnp.einsum("gh,ghpn->hpn", weighting, group_states, precision=HIGHEST_PREC)
    carried = jnp.exp(cumulative)[:, :, None] * jnp.einsum(
        "hpn,tn->thp", entering, out_float, precision=HIGHEST_PREC
    )
    ssm_out = inside + carried + skip_gain[None, :, None] * inputs_f
    gated_out = ssm_out.reshape(tok_rows, head_count * head_width) * jax.nn.silu(
        gate_input.astype(jnp.float32)
    )
    squares = lax.psum(jnp.sum(gated_out * gated_out, axis=1), DEV)
    mixed_rows = (
        gated_out * lax.rsqrt(squares[:, None] / inner_dim + EPSILON) * norm_gain[None, :]
    ).astype(jnp.bfloat16)
    gathered = lax.all_gather(mixed_rows, DEV, axis=0)
    projected = jnp.einsum(
        "dtc,dcf->tf",
        gathered,
        out_proj.reshape(dev_count, -1, out_proj.shape[1]),
        preferred_element_type=jnp.float32,
    ).astype(jnp.bfloat16)
    mamba_out = lax.all_to_all(projected, DEV, split_axis=0, concat_axis=1, tiled=True)
    hidden_res = (residual.astype(jnp.float32) + mamba_out.astype(jnp.float32)).astype(jnp.bfloat16)
    hidden_float = hidden_res.astype(jnp.float32)
    normed = rms_scale(hidden_float, ffn_gain).astype(jnp.bfloat16)
    logits = jnp.dot(normed.astype(jnp.float32), router, precision=HIGHEST_PREC)
    expert_ids = jnp.arange(experts, dtype=jnp.int32)[None, :]
    first_logit = jnp.sum(logits * (routes[:, 0:1] == expert_ids).astype(jnp.float32), axis=1)
    second_logit = jnp.sum(logits * (routes[:, 1:2] == expert_ids).astype(jnp.float32), axis=1)
    first_prob = jax.nn.sigmoid(first_logit - second_logit)
    second_prob = 1.0 - first_prob
    placed = slot_tables(routes[None], experts, slot_cap)[0]
    filled = jnp.sum(placed, axis=1)
    outgoing = jnp.dot(
        filled.T.astype(jnp.bfloat16), normed, preferred_element_type=jnp.float32
    ).astype(jnp.bfloat16)
    outgoing = outgoing.reshape(experts, slot_cap, model_dim)
    arrived = lax.all_to_all(outgoing, "grp", split_axis=0, concat_axis=0, tiled=True)
    all_rows = lax.all_gather(arrived, DEV, axis=0, tiled=True).reshape(-1, model_dim)
    gate_act = jnp.dot(all_rows, gate_weight[0], preferred_element_type=jnp.float32)
    up_act = jnp.dot(all_rows, up_weight[0], preferred_element_type=jnp.float32)
    hidden = (jax.nn.silu(gate_act) * up_act).astype(jnp.bfloat16)
    summed = sum_by_axis(jnp.dot(hidden, down_weight[0], preferred_element_type=jnp.float32), DEV)
    returned = lax.all_to_all(
        summed.astype(jnp.bfloat16).reshape(experts, slot_cap, model_dim),
        "grp",
        split_axis=0,
        concat_axis=0,
        tiled=True,
    )
    weights = first_prob[:, None] * placed[:, 0, :] + second_prob[:, None] * placed[:, 1, :]
    contrib = jnp.dot(
        weights,
        returned.reshape(group_slots, model_dim).astype(jnp.float32),
        precision=HIGHEST_PREC,
    )
    return (hidden_float + contrib).astype(jnp.bfloat16)


def solution(mesh):
    torus = Mesh(mesh.devices.reshape(mesh.shape["grp"], 4, 8), ("grp", "dev_0", "dev_1"))
    in_specs = (
        P("grp", DEV),
        P("grp", DEV),
        P("grp", DEV),
        P(DEV),
        P("grp", None),
        P("grp", None),
        P(DEV),
        P(DEV),
        P(None, DEV),
        P(GRP_DEV, None),
        P(),
        P(),
        P(GRP_DEV, None),
        P("grp", None, DEV),
        P("grp", None, DEV),
        P("grp", DEV, None),
    )
    out_specs = P(GRP_DEV, None)
    return jax.shard_map(
        shards, mesh=torus, in_specs=in_specs, out_specs=out_specs, check_vma=False
    )
```

profile of v0, /device:TPU:1, one launch (start us, length us, event | category | flops | bytes accessed | tf_op | source)
XLA Modules:
  0.0 574.6 jit_solution(1486846018110611630)
XLA Ops:
  6.6 0.9 negate_bitcast_fusion
  7.5 0.6 reduce-window.6
  8.5 0.2 slice_reduce_fusion.1
  8.8 0.8 fusion.58
  9.5 0.9 copy.61
  10.5 1.0 convolution_convert_fusion.2
  11.7 26.0 %all_gather.12 = bf16[16,2,8193]{2,1,0:T(2,128)(2,1)S(1)} all-gather(bf16[1,2,8193]{2,1,0:T(2,128)(2,1)S(1)} %pad_maximum_fusion), channel_id=1, replica_groups=mesh['grp'=16,'dev_0'=4,'dev_1'=8] {'grp'}, dimensions={0}, use_global_device_ids=true | all-gather | bytes 557124 | tf_op jit(solution)/shard_map/all_gather | solution.py:16
  37.6 0.7 slice.40
  38.9 0.4 reshape.234
  39.3 1.1 fusion.59
  40.3 0.6 fusion.18
  40.9 0.2 fusion.4
  41.2 0.6 fusion.3
  42.0 61.3 %psum.7 = f32[256]{0:T(256)S(1)} all-reduce(f32[256]{0:T(256)S(1)} %multiply_reduce_fusion), channel_id=1, replica_groups=mesh['grp'=16,'dev_0'=4,'dev_1'=8] {'dev_0','dev_1'}, use_global_device_ids=true, to_apply=%region_5.6 | all-reduce | flops 256 | bytes 2048 | tf_op jit(solution)/shard_map/psum | solution.py:144
  103.4 0.7 multiply_convert_fusion
  104.7 81.8 %all-gather.6.cloned.1.call-done = bf16[8192,128]{1,0:T(8,128)(2,1)} async-done(((bf16[256,128]{1,0:T(8,128)(2,1)}), bf16[8192,128]{1,0:T(8,128)(2,1)}) %all-gather.6.cloned.1.call-update) | async-done | bytes 2097168 | tf_op jit(solution)/shard_map/all_gather | solution.py:148
  186.6 2.3 fusion.5
  189.1 0.7 reshape.251
  189.8 4.9 all-to-all-start
  194.9 8.6 %all-to-all-done = bf16[32,2,256]{2,1,0:T(2,128)(2,1)S(1)} async-done(((bf16[32,2,256]{2,1,0:T(2,128)(2,1)}), bf16[32,2,256]{2,1,0:T(2,128)(2,1)S(1)}, u32[]{:S(2)}, u32[]{:S(2)}) %all-to-all-start) | async-done | bytes 32800 | tf_op jit(solution)/shard_map/all_to_all | solution.py:155
  203.9 0.2 convolution_convert_fusion.1
  204.3 22.8 %all_to_all.23 = bf16[16,2,2048]{2,1,0:T(2,128)(2,1)} all-to-all(bf16[16,2,2048]{2,1,0:T(2,128)(2,1)S(1)} %reshape.237), channel_id=1, replica_groups=mesh['grp'=16,'dev_0'=4,'dev_1'=8] {'grp'}, dimensions={0} | all-to-all | bytes 262144 | tf_op jit(solution)/shard_map/all_to_all | solution.py:171
  227.1 73.9 %all-gather.4.cloned.1.call-done = bf16[512,2,2048]{2,1,0:T(2,128)(2,1)} async-done(((bf16[16,2,2048]{2,1,0:T(2,128)(2,1)}), bf16[512,2,2048]{2,1,0:T(2,128)(2,1)}) %all-gather.4.cloned.1.call-update) | async-done | bytes 4194320 | tf_op jit(solution)/shard_map/all_gather | solution.py:172
  301.0 7.2 %reshape.238 = bf16[1024,2048]{1,0:T(8,128)(2,1)} reshape(bf16[512,2,2048]{2,1,0:T(2,128)(2,1)} %all-gather.4.cloned.1.call-done) | data formatting | bytes 8388608 | tf_op jit(solution)/shard_map/reshape | solution.py:172
  308.2 4.5 fusion.9
  312.8 9.1 %convolution_convert_fusion = bf16[1024,2048]{1,0:T(8,128)(2,1)} fusion(bf16[1024,2048]{1,0:T(8,128)(2,1)} %reshape.238, bf16[1,256,2048]{2,1,0:T(8,128)(2,1)S(1)} %copy-done, bf16[1,2048,256]{2,1,0:T(8,128)(2,1)} %param.30, f32[1024,256]{1,0:T(8,128)} %fusion.9), kind=kOutput, calls=%fused_computation | convolution fusion | flops 2151153664 | bytes 11534336 | tf_op jit(solution)/shard_map/dot_general | solution.py:176
  322.0 222.0 %reduce-scatter.2.cloned.1.call-done = bf16[32,2048]{1,0:T(8,128)(2,1)} async-done(((bf16[1024,2048]{1,0:T(8,128)(2,1)}), bf16[32,2048]{1,0:T(8,128)(2,1)}) %reduce-scatter.2.cloned.1.call-update) | async-done | bytes 131088 | tf_op jit(solution)/shard_map/reduce_scatter | solution.py:48
  544.0 1.7 reshape.239
  545.6 12.4 %all-to-all-start.2 = ((bf16[16,2,2048]{2,1,0:T(2,128)(2,1)}), bf16[16,2,2048]{2,1,0:T(2,128)(2,1)S(1)}, u32[]{:S(2)}, u32[]{:S(2)}) async-start(bf16[16,2,2048]{2,1,0:T(2,128)(2,1)} %reshape.239), calls=%async_computation.3 | async-start | bytes 262144 | tf_op jit(solution)/shard_map/all_to_all | solution.py:177
  558.0 0.3 select_reduce_fusion.2
  558.4 8.8 %all-to-all-done.2 = bf16[16,2,2048]{2,1,0:T(2,128)(2,1)S(1)} async-done(((bf16[16,2,2048]{2,1,0:T(2,128)(2,1)}), bf16[16,2,2048]{2,1,0:T(2,128)(2,1)S(1)}, u32[]{:S(2)}, u32[]{:S(2)}) %all-to-all-start.2) | async-done | bytes 131104 | tf_op jit(solution)/shard_map/all_to_all | solution.py:177
  567.2 0.9 fusion
  (72 shorter events, 3.0 us)
Async XLA Ops:
  6.5 306.2 %copy-start = (bf16[1,256,2048]{2,1,0:T(8,128)(2,1)S(1)}, bf16[1,256,2048]{2,1,0:T(8,128)(2,1)}, u32[]{:S(2)}) copy-start(bf16[1,256,2048]{2,1,0:T(8,128)(2,1)} %param.31) | copy-start | bytes 3145732
  6.5 34.6 %copy-start.6 = (f32[256,2]{0,1:T(2,128)S(1)}, f32[256,2]{0,1:T(2,128)}, u32[]{:S(2)}) copy-start(f32[256,2]{0,1:T(2,128)} %param.18) | copy-start | bytes 6148
  6.5 34.4 %copy-start.3 = (bf16[256,128]{1,0:T(8,128)(2,1)S(1)}, bf16[256,128]{1,0:T(8,128)(2,1)}, u32[]{:S(2)}) copy-start(bf16[256,128]{1,0:T(8,128)(2,1)} %param.21) | copy-start | bytes 196612
  6.5 34.6 %copy-start.11 = (f32[2]{0:T(128)S(1)}, f32[2]{0:T(128)}, u32[]{:S(2)}) copy-start(f32[2]{0:T(128)} %param.22) | copy-start | bytes 28
  6.5 35.3 %copy-start.2 = (bf16[256,128]{1,0:T(8,128)(2,1)S(1)}, bf16[256,128]{1,0:T(8,128)(2,1)}, u32[]{:S(2)}) copy-start(bf16[256,128]{1,0:T(8,128)(2,1)} %param.17) | copy-start | bytes 196612
  6.5 96.8 %copy-start.8 = (f32[128]{0:T(128)S(1)}, f32[128]{0:T(128)}, u32[]{:S(2)}) copy-start(f32[128]{0:T(128)} %param.23) | copy-start | bytes 1540
  6.6 97.5 %copy-start.7 = (s32[8,2]{0,1:T(2,128)S(1)}, s32[8,2]{0,1:T(2,128)}, u32[]{:S(2)}) copy-start(s32[8,2]{0,1:T(2,128)} %param.28) | copy-start | bytes 196
  6.6 180.0 %copy-start.1 = (bf16[4096,64]{0,1:T(8,128)(2,1)S(1)}, bf16[4096,64]{0,1:T(8,128)(2,1)}, u32[]{:S(2)}) copy-start(bf16[4096,64]{0,1:T(8,128)(2,1)} %param.24) | copy-start | bytes 1572868
  6.6 180.0 %all-gather.6.cloned.1.call-start = ((), (), s32[]{:S(2)}) async-start(), calls=%async_computation.6 | async-start | bytes 2162688 | tf_op jit(solution)/shard_map/all_gather | solution.py:148
  38.3 165.4 %copy-start.4 = (bf16[8,2048]{1,0:T(8,128)(2,1)S(1)}, bf16[8,2048]{1,0:T(8,128)(2,1)}, u32[]{:S(2)}) copy-start(bf16[8,2048]{1,0:T(8,128)(2,1)} %param.25) | copy-start | bytes 98308
  38.7 165.2 %copy-start.5 = (f32[2048]{0:T(1024)S(1)}, f32[2048]{0:T(1024)}, u32[]{:S(2)}) copy-start(f32[2048]{0:T(1024)} %param.26) | copy-start | bytes 24580
  189.8 13.7 %all-to-all-start = ((bf16[32,2,256]{2,1,0:T(2,128)(2,1)}), bf16[32,2,256]{2,1,0:T(2,128)(2,1)S(1)}, u32[]{:S(2)}, u32[]{:S(2)}) async-start(bf16[32,2,256]{2,1,0:T(2,128)(2,1)} %reshape.251), calls=%async_computation | async-start | bytes 65536 | tf_op jit(solution)/shard_map/all_to_all | solution.py:155
  194.7 106.3 %all-gather.4.cloned.1.call-start = ((), (), s32[]{:S(2)}) async-start(), calls=%async_computation.4 | async-start | bytes 4325376 | tf_op jit(solution)/shard_map/all_gather | solution.py:172
  227.1 81.2 %copy-start.9 = (bf16[1,2048,256]{2,1,0:T(8,128)(2,1)S(1)}, bf16[1,2048,256]{2,1,0:T(8,128)(2,1)}, u32[]{:S(2)}) copy-start(bf16[1,2048,256]{2,1,0:T(8,128)(2,1)} %param.29) | copy-start | bytes 3145732
  227.1 316.9 %reduce-scatter.2.cloned.1.call-start = ((), (), s32[]{:S(2)}) async-start(), calls=%async_computation.5 | async-start | bytes 4325376 | tf_op jit(solution)/shard_map/reduce_scatter | solution.py:48
  321.9 236.1 %copy-start.10 = (f32[2048,16]{0,1:T(8,128)S(1)}, f32[2048,16]{0,1:T(8,128)}, u32[]{:S(2)}) copy-start(f32[2048,16]{0,1:T(8,128)} %param.27) | copy-start | bytes 393220
  545.6 21.6 %all-to-all-start.2 = ((bf16[16,2,2048]{2,1,0:T(2,128)(2,1)}), bf16[16,2,2048]{2,1,0:T(2,128)(2,1)S(1)}, u32[]{:S(2)}, u32[]{:S(2)}) async-start(bf16[16,2,2048]{2,1,0:T(2,128)(2,1)} %reshape.239), calls=%async_computation.3 | async-start | bytes 262144 | tf_op jit(solution)/shard_map/all_to_all | solution.py:177
Sparse Core Ops, SparseCore 0:
  104.2 82.3 all-gather.5
  227.2 73.7 all-gather.3
  322.0 221.9 reduce-scatter.1
where the time goes:
time: 575 us
  waiting for transfers between devices  395 us (69%)
  blocking collectives  110 us (19%)
  matrix products  20.9 us (4%)
  starting transfers between devices  17.4 us (3%)
  between operations  13.4 us (2%)
  local copies, waits for them, and re-layouts  13.3 us (2%)
    reduce_scatter x1, waiting for transfers between devices, sum_by_axis(): total = lax.psum_scatter(total, axes, scatter_dimension=0, tiled=True)  222 us
    all_gather x1, waiting for transfers between devices, shards(): gathered = lax.all_gather(mixed_rows, DEV, axis=0)  81.8 us
    all_gather x1, waiting for transfers between devices, shards(): lax.all_gather(arrived, DEV, axis=0, tiled=True).reshape(-1, model_dim)  73.9 us
    psum x1, blocking collectives, shards(): squares = lax.psum(jnp.sum(gated_out * gated_out, axis=1), DEV)  61.3 us
    all_gather x1, blocking collectives, side_by_side(): lax.all_gather(both, axis, axis=dim, tiled=True)  26 us
    all_to_all x1, blocking collectives, shards(): lax.all_to_all(outgoing, 'grp', split_axis=0, concat_axis=0, tiled=True)  22.8 us
    all_to_all x1, starting transfers between devices, shards(): lax.all_to_all(summed.astype(jnp.bfloat16).reshape(experts, slot_cap, mod...  12.4 us
  transfers between devices with their start and end apart: 5, of which 5 were waited for; matrix products, arithmetic and copies ran while one was open for 0% of the time, Pallas kernels for 0%

commit v1 on v0

--- a/solution.py
+++ b/solution.py
@@ -141,7 +141,7 @@
     gated_out = ssm_out.reshape(tok_rows, head_count * head_width) * jax.nn.silu(
         gate_input.astype(jnp.float32)
     )
-    squares = lax.psum(jnp.sum(gated_out * gated_out, axis=1), DEV)
+    squares = lax.psum(lax.psum(jnp.sum(gated_out * gated_out, axis=1), "dev_0"), "dev_1")
     mixed_rows = (
         gated_out * lax.rsqrt(squares[:, None] / inner_dim + EPSILON) * norm_gain[None, :]
     ).astype(jnp.bfloat16)

time: 575 us -> 531 us (0.923)
  blocking collectives: 110 us -> 71.3 us
  waiting for transfers between devices: 395 us -> 389 us
    psum x1 -> x2, blocking collectives: 61.3 us -> 22.6 us  [the longest x1 14.1 us: shards(): lax.psum(lax.psum(jnp.sum(gated_out * gated_out, axis=1), 'dev_0'), 'dev_1')]
where the time goes in v1:
time: 531 us; the launch traced here: 530 us
  waiting for transfers between devices  389 us (73%)
  blocking collectives  71.3 us (13%)
  matrix products  20.9 us (4%)
  starting transfers between devices  17.5 us (3%)
  between operations  13.4 us (3%)
  local copies, waits for them, and re-layouts  13.3 us (3%)
    reduce_scatter x1, waiting for transfers between devices, sum_by_axis(): total = lax.psum_scatter(total, axes, scatter_dimension=0, tiled=True)  222 us
    all_gather x1, waiting for transfers between devices, shards(): gathered = lax.all_gather(mixed_rows, DEV, axis=0)  76.1 us
    all_gather x1, waiting for transfers between devices, shards(): lax.all_gather(arrived, DEV, axis=0, tiled=True).reshape(-1, model_dim)  73.9 us
    all_gather x1, blocking collectives, side_by_side(): lax.all_gather(both, axis, axis=dim, tiled=True)  26 us
    all_to_all x1, blocking collectives, shards(): lax.all_to_all(outgoing, 'grp', split_axis=0, concat_axis=0, tiled=True)  22.8 us
    psum x1, blocking collectives, shards(): lax.psum(lax.psum(jnp.sum(gated_out * gated_out, axis=1), 'dev_0'), 'dev_1')  14.1 us
    all_to_all x1, starting transfers between devices, shards(): lax.all_to_all(summed.astype(jnp.bfloat16).reshape(experts, slot_cap, mod...  12.4 us
  transfers between devices with their start and end apart: 5, of which 5 were waited for; matrix products, arithmetic and copies ran while one was open for 0% of the time, Pallas kernels for 0%

profile of v1, /device:TPU:1, one launch (start us, length us, event | category | flops | bytes accessed | tf_op | source)
XLA Modules:
  0.0 530.2 jit_solution(4325999446206772022)
XLA Ops:
  6.6 0.9 negate_bitcast_fusion
  7.5 0.6 reduce-window.6
  8.8 0.8 fusion.58
  9.5 0.9 copy.61
  10.5 1.0 convolution_convert_fusion.2
  11.7 26.0 %all_gather.12 = bf16[16,2,8193]{2,1,0:T(2,128)(2,1)S(1)} all-gather(bf16[1,2,8193]{2,1,0:T(2,128)(2,1)S(1)} %pad_maximum_fusion), channel_id=1, replica_groups=mesh['grp'=16,'dev_0'=4,'dev_1'=8] {'grp'}, dimensions={0}, use_global_device_ids=true | all-gather | bytes 557124 | tf_op jit(solution)/shard_map/all_gather | solution.py:16
  37.6 0.7 slice.40
  38.9 0.4 reshape.234
  39.3 1.1 fusion.59
  40.3 0.6 fusion.18
  40.9 0.2 fusion.4
  41.2 0.6 fusion.3
  42.0 8.5 %psum.14 = f32[256]{0:T(256)S(1)} all-reduce(f32[256]{0:T(256)S(1)} %multiply_reduce_fusion), channel_id=1, replica_groups=mesh['grp'=16,'dev_0'=4,'dev_1'=8] {'dev_0'}, use_global_device_ids=true, to_apply=%region_5.6 | all-reduce | flops 256 | bytes 2048 | tf_op jit(solution)/shard_map/psum | solution.py:144
  50.5 14.1 %psum.15 = f32[256]{0:T(256)S(1)} all-reduce(f32[256]{0:T(256)S(1)} %psum.14), channel_id=1, replica_groups=mesh['grp'=16,'dev_0'=4,'dev_1'=8] {'dev_1'}, use_global_device_ids=true, to_apply=%region_6.7 | all-reduce | flops 256 | bytes 2048 | tf_op jit(solution)/shard_map/psum | solution.py:144
  64.6 0.7 multiply_convert_fusion
  66.0 76.1 %all-gather.6.cloned.1.call-done = bf16[8192,128]{1,0:T(8,128)(2,1)} async-done(((bf16[256,128]{1,0:T(8,128)(2,1)}), bf16[8192,128]{1,0:T(8,128)(2,1)}) %all-gather.6.cloned.1.call-update) | async-done | bytes 2097168 | tf_op jit(solution)/shard_map/all_gather | solution.py:148
  142.2 2.3 fusion.5
  144.6 0.7 reshape.251
  145.4 4.9 all-to-all-start
  150.5 8.6 %all-to-all-done = bf16[32,2,256]{2,1,0:T(2,128)(2,1)S(1)} async-done(((bf16[32,2,256]{2,1,0:T(2,128)(2,1)}), bf16[32,2,256]{2,1,0:T(2,128)(2,1)S(1)}, u32[]{:S(2)}, u32[]{:S(2)}) %all-to-all-start) | async-done | bytes 32800 | tf_op jit(solution)/shard_map/all_to_all | solution.py:155
  159.5 0.2 convolution_convert_fusion.1
  159.9 22.8 %all_to_all.23 = bf16[16,2,2048]{2,1,0:T(2,128)(2,1)} all-to-all(bf16[16,2,2048]{2,1,0:T(2,128)(2,1)S(1)} %reshape.237), channel_id=1, replica_groups=mesh['grp'=16,'dev_0'=4,'dev_1'=8] {'grp'}, dimensions={0} | all-to-all | bytes 262144 | tf_op jit(solution)/shard_map/all_to_all | solution.py:171
  182.7 73.9 %all-gather.4.cloned.1.call-done = bf16[512,2,2048]{2,1,0:T(2,128)(2,1)} async-done(((bf16[16,2,2048]{2,1,0:T(2,128)(2,1)}), bf16[512,2,2048]{2,1,0:T(2,128)(2,1)}) %all-gather.4.cloned.1.call-update) | async-done | bytes 4194320 | tf_op jit(solution)/shard_map/all_gather | solution.py:172
  256.6 7.2 %reshape.238 = bf16[1024,2048]{1,0:T(8,128)(2,1)} reshape(bf16[512,2,2048]{2,1,0:T(2,128)(2,1)} %all-gather.4.cloned.1.call-done) | data formatting | bytes 8388608 | tf_op jit(solution)/shard_map/reshape | solution.py:172
  263.8 4.5 fusion.9
  268.3 9.1 %convolution_convert_fusion = bf16[1024,2048]{1,0:T(8,128)(2,1)} fusion(bf16[1024,2048]{1,0:T(8,128)(2,1)} %reshape.238, bf16[1,256,2048]{2,1,0:T(8,128)(2,1)S(1)} %copy-done, bf16[1,2048,256]{2,1,0:T(8,128)(2,1)} %param.30, f32[1024,256]{1,0:T(8,128)} %fusion.9), kind=kOutput, calls=%fused_computation | convolution fusion | flops 2151153664 | bytes 11534336 | tf_op jit(solution)/shard_map/dot_general | solution.py:176
  277.5 222.0 %reduce-scatter.2.cloned.1.call-done = bf16[32,2048]{1,0:T(8,128)(2,1)} async-done(((bf16[1024,2048]{1,0:T(8,128)(2,1)}), bf16[32,2048]{1,0:T(8,128)(2,1)}) %reduce-scatter.2.cloned.1.call-update) | async-done | bytes 131088 | tf_op jit(solution)/shard_map/reduce_scatter | solution.py:48
  499.5 1.7 reshape.239
  501.2 12.4 %all-to-all-start.2 = ((bf16[16,2,2048]{2,1,0:T(2,128)(2,1)}), bf16[16,2,2048]{2,1,0:T(2,128)(2,1)S(1)}, u32[]{:S(2)}, u32[]{:S(2)}) async-start(bf16[16,2,2048]{2,1,0:T(2,128)(2,1)} %reshape.239), calls=%async_computation.3 | async-start | bytes 262144 | tf_op jit(solution)/shard_map/all_to_all | solution.py:177
  513.6 0.3 select_reduce_fusion.2
  513.9 8.8 %all-to-all-done.2 = bf16[16,2,2048]{2,1,0:T(2,128)(2,1)S(1)} async-done(((bf16[16,2,2048]{2,1,0:T(2,128)(2,1)}), bf16[16,2,2048]{2,1,0:T(2,128)(2,1)S(1)}, u32[]{:S(2)}, u32[]{:S(2)}) %all-to-all-start.2) | async-done | bytes 131104 | tf_op jit(solution)/shard_map/all_to_all | solution.py:177
  522.8 0.9 fusion
  (73 shorter events, 3.2 us)
Async XLA Ops:
  6.5 261.8 %copy-start = (bf16[1,256,2048]{2,1,0:T(8,128)(2,1)S(1)}, bf16[1,256,2048]{2,1,0:T(8,128)(2,1)}, u32[]{:S(2)}) copy-start(bf16[1,256,2048]{2,1,0:T(8,128)(2,1)} %param.31) | copy-start | bytes 3145732
  6.5 34.6 %copy-start.6 = (f32[256,2]{0,1:T(2,128)S(1)}, f32[256,2]{0,1:T(2,128)}, u32[]{:S(2)}) copy-start(f32[256,2]{0,1:T(2,128)} %param.18) | copy-start | bytes 6148
  6.5 34.4 %copy-start.3 = (bf16[256,128]{1,0:T(8,128)(2,1)S(1)}, bf16[256,128]{1,0:T(8,128)(2,1)}, u32[]{:S(2)}) copy-start(bf16[256,128]{1,0:T(8,128)(2,1)} %param.21) | copy-start | bytes 196612
  6.5 34.6 %copy-start.11 = (f32[2]{0:T(128)S(1)}, f32[2]{0:T(128)}, u32[]{:S(2)}) copy-start(f32[2]{0:T(128)} %param.22) | copy-start | bytes 28
  6.5 35.3 %copy-start.2 = (bf16[256,128]{1,0:T(8,128)(2,1)S(1)}, bf16[256,128]{1,0:T(8,128)(2,1)}, u32[]{:S(2)}) copy-start(bf16[256,128]{1,0:T(8,128)(2,1)} %param.17) | copy-start | bytes 196612
  6.5 58.1 %copy-start.8 = (f32[128]{0:T(128)S(1)}, f32[128]{0:T(128)}, u32[]{:S(2)}) copy-start(f32[128]{0:T(128)} %param.23) | copy-start | bytes 1540
  6.6 58.8 %copy-start.7 = (s32[8,2]{0,1:T(2,128)S(1)}, s32[8,2]{0,1:T(2,128)}, u32[]{:S(2)}) copy-start(s32[8,2]{0,1:T(2,128)} %param.28) | copy-start | bytes 196
  6.6 135.6 %copy-start.1 = (bf16[4096,64]{0,1:T(8,128)(2,1)S(1)}, bf16[4096,64]{0,1:T(8,128)(2,1)}, u32[]{:S(2)}) copy-start(bf16[4096,64]{0,1:T(8,128)(2,1)} %param.24) | copy-start | bytes 1572868
  6.6 135.6 %all-gather.6.cloned.1.call-start = ((), (), s32[]{:S(2)}) async-start(), calls=%async_computation.6 | async-start | bytes 2162688 | tf_op jit(solution)/shard_map/all_gather | solution.py:148
  38.3 121.0 %copy-start.4 = (bf16[8,2048]{1,0:T(8,128)(2,1)S(1)}, bf16[8,2048]{1,0:T(8,128)(2,1)}, u32[]{:S(2)}) copy-start(bf16[8,2048]{1,0:T(8,128)(2,1)} %param.25) | copy-start | bytes 98308
  38.7 120.8 %copy-start.5 = (f32[2048]{0:T(1024)S(1)}, f32[2048]{0:T(1024)}, u32[]{:S(2)}) copy-start(f32[2048]{0:T(1024)} %param.26) | copy-start | bytes 24580
  145.4 13.7 %all-to-all-start = ((bf16[32,2,256]{2,1,0:T(2,128)(2,1)}), bf16[32,2,256]{2,1,0:T(2,128)(2,1)S(1)}, u32[]{:S(2)}, u32[]{:S(2)}) async-start(bf16[32,2,256]{2,1,0:T(2,128)(2,1)} %reshape.251), calls=%async_computation | async-start | bytes 65536 | tf_op jit(solution)/shard_map/all_to_all | solution.py:155
  150.3 106.3 %all-gather.4.cloned.1.call-start = ((), (), s32[]{:S(2)}) async-start(), calls=%async_computation.4 | async-start | bytes 4325376 | tf_op jit(solution)/shard_map/all_gather | solution.py:172
  182.7 81.2 %copy-start.9 = (bf16[1,2048,256]{2,1,0:T(8,128)(2,1)S(1)}, bf16[1,2048,256]{2,1,0:T(8,128)(2,1)}, u32[]{:S(2)}) copy-start(bf16[1,2048,256]{2,1,0:T(8,128)(2,1)} %param.29) | copy-start | bytes 3145732
  182.7 316.8 %reduce-scatter.2.cloned.1.call-start = ((), (), s32[]{:S(2)}) async-start(), calls=%async_computation.5 | async-start | bytes 4325376 | tf_op jit(solution)/shard_map/reduce_scatter | solution.py:48
  277.4 236.1 %copy-start.10 = (f32[2048,16]{0,1:T(8,128)S(1)}, f32[2048,16]{0,1:T(8,128)}, u32[]{:S(2)}) copy-start(f32[2048,16]{0,1:T(8,128)} %param.27) | copy-start | bytes 393220
  501.2 21.6 %all-to-all-start.2 = ((bf16[16,2,2048]{2,1,0:T(2,128)(2,1)}), bf16[16,2,2048]{2,1,0:T(2,128)(2,1)S(1)}, u32[]{:S(2)}, u32[]{:S(2)}) async-start(bf16[16,2,2048]{2,1,0:T(2,128)(2,1)} %reshape.239), calls=%async_computation.3 | async-start | bytes 262144 | tf_op jit(solution)/shard_map/all_to_all | solution.py:177
Sparse Core Ops, SparseCore 0:
  65.5 76.6 all-gather.5
  182.8 73.7 all-gather.3
  277.6 221.8 reduce-scatter.1
